TPU v7x, 256 devices: a whole 4x4x8 slice. The times are simulated.
256 devices in a mesh: grp: 4 (over y), mdl: 64 (over z, x, core).
Axes of the slice: x: 4, y: 4, z: 8, core: 2. Of those that a mesh axis runs over, the one named last changes fastest.
Arguments:
- pol_hidden: bfloat16 [1024, 4096], P(('grp', 'mdl')), may hold values from -6 to 6
- ref_hidden: bfloat16 [1024, 4096], P(('grp', 'mdl')), may hold values from -6 to 6
- pol_mlp_gain: bfloat16 [4096], replicated, may hold values from 0.099609375 to 1.8984375
- ref_mlp_gain: bfloat16 [4096], replicated, may hold values from 0.099609375 to 1.8984375
- pol_final_gain: bfloat16 [4096], replicated, may hold values from 0.099609375 to 1.8984375
- ref_final_gain: bfloat16 [4096], replicated, may hold values from 0.099609375 to 1.8984375
- pol_gate: bfloat16 [4096, 11008], P(None, 'mdl'), may hold values from -0.09375 to 0.09375
- pol_up: bfloat16 [4096, 11008], P(None, 'mdl'), may hold values from -0.09375 to 0.09375
- pol_down: bfloat16 [11008, 4096], P('mdl'), may hold values from -0.109375 to 0.109375
- ref_gate: bfloat16 [4096, 11008], P(None, 'mdl'), may hold values from -0.09375 to 0.09375
- ref_up: bfloat16 [4096, 11008], P(None, 'mdl'), may hold values from -0.09375 to 0.09375
- ref_down: bfloat16 [11008, 4096], P('mdl'), may hold values from -0.109375 to 0.109375
- pol_head: bfloat16 [64000, 4096], P(('grp', 'mdl')), may hold values from -20 to 20
- ref_head: bfloat16 [64000, 4096], P(('grp', 'mdl')), may hold values from -20 to 20
- token_ids: int32 [1024], replicated, may hold values from 0 to 63999
- lengths: int32 [16], replicated, may hold values from 1 to 160, 1024 in all
Outputs:
- pol_out: bfloat16 [1024, 4096], P(('grp', 'mdl'))
- ref_out: bfloat16 [1024, 4096], P(('grp', 'mdl'))
- rollout_ratio: float32 [16], replicated
Inputs may be any that keep to these rules, and one draw needn't show every extreme that they name: Rollout lengths sum to 1024; the longest is exactly 160.
All inputs are finite; a program needn't handle non-finite values.
Results may differ from a plain program's by a relative error of at most 0.012.
The roundings to bfloat16 on the way count: a program that leaves them out, or rounds other values in their place, can miss the bound.
Values may be sent and summed in bfloat16 or wider, within the bound.
No kernel may reach another device: no remote copies, remote signals or barrier semaphores. Data moves between devices by JAX's collectives and lax.ppermute only.
A program may use at most 128 MiB of HBM per device.

v0:
```python
import jax
import jax.numpy as jnp
from jax import lax
from jax.sharding import PartitionSpec as P


def rms_rows(rows, gain):
    values = rows.astype(jnp.float32)
    scale = lax.rsqrt(jnp.mean(values * values, axis=-1, keepdims=True) + 1e-05)
    return (values * scale * gain.astype(jnp.float32)).astype(jnp.bfloat16)


def mlp_partial(piece, gain, w_gate, w_up, w_down):
    normed = rms_rows(piece, gain)
    gate = jnp.dot(normed, w_gate, preferred_element_type=jnp.float32)
    upper = jnp.dot(normed, w_up, preferred_element_type=jnp.float32)
    hidden = (jax.nn.silu(gate) * upper).astype(jnp.bfloat16)
    return jnp.dot(hidden, w_down, preferred_element_type=jnp.float32)


def vocab_terms(token_rows, head_rows, targets, vocab):
    logits = jnp.einsum("td,vd->tv", token_rows, head_rows, preferred_element_type=jnp.float32)
    peak = jnp.max(logits, axis=1)
    total = jnp.sum(jnp.exp(logits - peak[:, None]), axis=1)
    target = jnp.sum(jnp.where(targets[:, None] == vocab[None, :], logits, 0.0), axis=1)
    return (peak, total, target)


def rollout_totals(log_ratio, positions, lengths):
    ends = jnp.cumsum(lengths)
    owner = jnp.sum((positions[:, None] >= ends[None, :]).astype(jnp.int32), axis=1)
    onehot = (owner[:, None] == jnp.arange(lengths.shape[0], dtype=jnp.int32)[None, :]).astype(
        jnp.float32
    )
    return jnp.sum(log_ratio[:, None] * onehot, axis=0)


def per_device(
    pol_hidden,
    ref_hidden,
    pol_mlp_gain,
    ref_mlp_gain,
    pol_final_gain,
    ref_final_gain,
    pol_gate,
    pol_up,
    pol_down,
    ref_gate,
    ref_up,
    ref_down,
    pol_head,
    ref_head,
    token_ids,
    lengths,
):
    rows = pol_hidden.shape[0]
    member = lax.axis_index("mdl")
    group = lax.axis_index("grp")
    members = lax.axis_size("mdl")
    both_in = lax.all_gather(jnp.stack([pol_hidden, ref_hidden]), "mdl", axis=1, tiled=True)
    partials = (
        mlp_partial(both_in[0], pol_mlp_gain, pol_gate, pol_up, pol_down),
        mlp_partial(both_in[1], ref_mlp_gain, ref_gate, ref_up, ref_down),
    )
    mixed = lax.psum(partials, "mdl")
    outs = [(both_in[i].astype(jnp.float32) + mixed[i]).astype(jnp.bfloat16) for i in range(2)]
    finals = jnp.stack([rms_rows(outs[0], pol_final_gain), rms_rows(outs[1], ref_final_gain)])
    own = [lax.dynamic_slice_in_dim(o, member * rows, rows, axis=0) for o in outs]
    every = lax.all_gather(finals, "grp", axis=1, tiled=True)
    voc_dev = pol_head.shape[0]
    positions = jnp.arange(every.shape[1], dtype=jnp.int32)
    vocab = (group * members + member) * voc_dev + jnp.arange(voc_dev, dtype=jnp.int32)
    pol_terms = vocab_terms(every[0], pol_head, token_ids, vocab)
    ref_terms = vocab_terms(every[1], ref_head, token_ids, vocab)
    peaks = lax.pmax(lax.pmax((pol_terms[0], ref_terms[0]), "mdl"), "grp")
    sums = lax.psum(
        lax.psum(
            (
                pol_terms[1] * jnp.exp(pol_terms[0] - peaks[0]),
                pol_terms[2],
                ref_terms[1] * jnp.exp(ref_terms[0] - peaks[1]),
                ref_terms[2],
            ),
            "mdl",
        ),
        "grp",
    )
    pol_logp = sums[1] - peaks[0] - jnp.log(sums[0])
    ref_logp = sums[3] - peaks[1] - jnp.log(sums[2])
    rollout_ratio = rollout_totals(pol_logp - ref_logp, positions, lengths)
    return (own[0], own[1], rollout_ratio)


def solution(mesh):
    placed = (
        P(("grp", "mdl"), None),
        P(("grp", "mdl"), None),
        P(),
        P(),
        P(),
        P(),
        P(None, "mdl"),
        P(None, "mdl"),
        P("mdl", None),
        P(None, "mdl"),
        P(None, "mdl"),
        P("mdl", None),
        P(("grp", "mdl"), None),
        P(("grp", "mdl"), None),
        P(),
        P(),
    )
    return jax.shard_map(
        per_device,
        mesh=mesh,
        in_specs=placed,
        out_specs=(P(("grp", "mdl"), None), P(("grp", "mdl"), None), P()),
        check_vma=False,
    )
```

profile of v0, /device:TPU:8, one launch (start us, length us, event | category | flops | bytes accessed | tf_op | source)
XLA Modules:
  0.0 921.6 jit_solution(18328997950964783200)
XLA Ops:
  7.2 1.0 pad_maximum_fusion.1
  8.2 0.7 copy.28
  9.0 1.3 convert_element_type.62
  10.3 0.7 convert_element_type.68
  11.0 81.7 %all-gather.3.cloned.1.call-done = bf16[2,256,4096]{2,0,1:T(2,128)(2,1)} async-done(((bf16[2,4,4096]{2,0,1:T(2,128)(2,1)}), bf16[2,256,4096]{2,0,1:T(2,128)(2,1)}) %all-gather.3.cloned.1.call-update) | async-done | bytes 4194320 | tf_op jit(solution)/shard_map/all_gather | solution.py:60
  92.7 13.2 %fusion.48 = (bf16[1,256,4096]{2,0,1:T(2,128)(2,1)S(1)}, bf16[1,256,4096]{2,0,1:T(2,128)(2,1)S(1)}) fusion(bf16[2,256,4096]{2,0,1:T(2,128)(2,1)} %all-gather.3.cloned.1.call-done), kind=kLoop, calls=%fused_computation.76 | loop fusion | bytes 8388608 | tf_op jit(solution)/shard_map/slice | solution.py:66
  105.9 6.7 fusion.8
  112.6 0.6 add_rsqrt_fusion.2
  113.2 0.6 copy-done.2
  113.9 1.6 fusion.30
  115.5 6.6 fusion.21
  122.1 3.7 fusion.26
  125.8 6.6 fusion.20
  133.1 201.9 %all-reduce.7.cloned.1.call-done = (f32[256,4096]{1,0:T(8,128)}, f32[256,4096]{1,0:T(8,128)}) async-done(((f32[256,4096]{1,0:T(8,128)}, f32[256,4096]{1,0:T(8,128)}), (f32[256,4096]{1,0:T(8,128)}, f32[256,4096]{1,0:T(8,128)})) %all-reduce.7.cloned.1.call-update) | async-done | bytes 8388624 | tf_op jit(solution)/shard_map/psum | solution.py:65
  335.0 3.8 fusion.2
  338.9 0.8 copy-done.5
  339.7 0.8 fusion.5
  340.6 0.6 fusion.16
  341.2 0.7 copy-done.4
  342.5 2.3 pad_maximum_fusion
  345.8 1.5 constant_dynamic-slice_fusion.1
  347.3 1.5 constant_dynamic-slice_fusion
  348.8 151.6 %all-gather.5.cloned.1.call-done = bf16[2,1024,4096]{2,1,0:T(8,128)(2,1)} async-done(((bf16[2,256,4096]{2,1,0:T(8,128)(2,1)}), bf16[2,1024,4096]{2,1,0:T(8,128)(2,1)}) %all-gather.5.cloned.1.call-update) | async-done | bytes 16777232 | tf_op jit(solution)/shard_map/all_gather | solution.py:69
  500.4 5.9 fusion.49
  506.3 2.2 copy-done.14
  509.2 3.4 fusion.50
  512.5 131.0 %all-reduce.2 = (f32[1024]{0:T(1024)S(1)}, f32[1024]{0:T(1024)S(1)}) all-reduce(f32[1024]{0:T(1024)S(1)} %get-tuple-element.35, f32[1024]{0:T(1024)S(1)} %get-tuple-element.33), channel_id=1, replica_groups=mesh['grp'=4,'mdl'=64] {'mdl'}, use_global_device_ids=true, to_apply=%region_21.22 | all-reduce | flops 2048 | bytes 16384 | tf_op jit(solution)/shard_map/pmax | solution.py:75
  643.5 8.4 all-reduce.4
  652.0 1.7 fusion.22
  653.7 246.2 %all-reduce = (f32[1024]{0:T(1024)S(1)}, f32[1024]{0:T(1024)S(1)}, f32[1024]{0:T(1024)S(1)}, f32[1024]{0:T(1024)S(1)}) all-reduce(f32[1024]{0:T(1024)S(1)} %exponential_multiply_fusion, f32[1024]{0:T(1024)S(1)} %get-tuple-element.8, f32[1024]{0:T(1024)S(1)} %exponential_multiply_fusion.1, ...), channel_id=1, replica_groups=mesh['grp'=4,'mdl'=64] {'mdl'}, use_global_device_ids=true, to_apply=%region_24.25 | all-reduce | flops 4096 | bytes 32768 | tf_op jit(solution)/shard_map/psum | solution.py:77
  899.9 14.6 %all-reduce.3 = (f32[1024]{0:T(1024)S(1)}, f32[1024]{0:T(1024)S(1)}, f32[1024]{0:T(1024)S(1)}, f32[1024]{0:T(1024)S(1)}) all-reduce(f32[1024]{0:T(1024)S(1)} %get-tuple-element.9, f32[1024]{0:T(1024)S(1)} %get-tuple-element.10, f32[1024]{0:T(1024)S(1)} %get-tuple-element.11, ...), channel_id=1, replica_groups=mesh['grp'=4,'mdl'=64] {'grp'}, use_global_device_ids=true, to_apply=%region_25.26 | all-reduce | flops 4096 | bytes 32768 | tf_op jit(solution)/shard_map/psum | solution.py:76
  914.5 0.6 select_reduce_fusion
  (50 shorter events, 3.1 us)
Async XLA Ops:
  7.2 493.2 %copy-start = (bf16[250,4096]{1,0:T(8,128)(2,1)S(1)}, bf16[250,4096]{1,0:T(8,128)(2,1)}, u32[]{:S(2)}) copy-start(bf16[250,4096]{1,0:T(8,128)(2,1)} %param.28) | copy-start | bytes 6144004
  7.2 85.5 %all-gather.3.cloned.1.call-start = ((), (), s32[]{:S(2)}) async-start(), calls=%async_computation | async-start | bytes 4259840 | tf_op jit(solution)/shard_map/all_gather | solution.py:60
  8.9 326.1 %all-reduce.7.cloned.1.call-start = ((), (), s32[]{:S(2)}) async-start(), calls=%async_computation.2 | async-start | bytes 16777216 | tf_op jit(solution)/shard_map/psum | solution.py:65
  105.9 8.0 copy-start.8
  105.9 8.0 copy-start.16
  112.6 1.3 copy-start.2
  112.6 1.3 copy-start.12
  113.9 1.6 copy-start.6
  122.1 3.7 copy-start.7
  132.4 0.7 copy-start.9
  132.4 0.7 copy-start.10
  132.4 368.0 %all-gather.5.cloned.1.call-start = ((), (), s32[]{:S(2)}) async-start(), calls=%async_computation.1 | async-start | bytes 20971520 | tf_op jit(solution)/shard_map/all_gather | solution.py:69
  335.0 3.9 copy-start.1
  335.0 4.7 copy-start.5
  338.9 3.0 copy-start.3
  340.6 1.3 copy-start.4
  344.8 0.7 copy-start.13
  500.4 8.2 copy-start.14
  500.4 8.7 copy-start.15
  509.2 142.8 %copy-start.11 = (s32[1024]{0:T(1024)S(1)}, s32[1024]{0:T(1024)}, u32[]{:S(2)}) copy-start(s32[1024]{0:T(1024)} %param.30) | copy-start | bytes 12292
Sparse Core Ops, SparseCore 0:
  10.8 81.8 all-gather.2
  132.5 202.4 all-reduce.6
  345.0 155.3 all-gather.4
where the time goes:
time: 922 us
  waiting for transfers between devices  435 us (47%)
  blocking collectives  400 us (43%)
  matrix products  27.8 us (3%)
  local copies, waits for them, and re-layouts  23 us (2%)
  other arithmetic  21.2 us (2%)
  between operations  13.9 us (2%)
    psum x1, blocking collectives, per_device(): lax.psum((pol_terms[1] * jnp.exp(pol_terms[0] - peaks[0]), pol_terms[2],...  246 us
    psum x1, waiting for transfers between devices, per_device(): mixed = lax.psum(partials, 'mdl')  202 us
    all_gather x1, waiting for transfers between devices, per_device(): every = lax.all_gather(finals, 'grp', axis=1, tiled=True)  152 us
    pmax x2, blocking collectives, per_device(): peaks = lax.pmax(lax.pmax((pol_terms[0], ref_terms[0]), 'mdl'), 'grp')  139 us
    all_gather x1, waiting for transfers between devices, per_device(): lax.all_gather(jnp.stack([pol_hidden, ref_hidden]), 'mdl', axis=1, tiled=...  81.7 us
  transfers between devices with their start and end apart: 3, of which 3 were waited for; matrix products, arithmetic and copies ran while one was open for 1% of the time, Pallas kernels for 0%

commit v1 on v0

--- a/solution.py
+++ b/solution.py
@@ -57,7 +57,12 @@
     member = lax.axis_index("mdl")
     group = lax.axis_index("grp")
     members = lax.axis_size("mdl")
-    both_in = lax.all_gather(jnp.stack([pol_hidden, ref_hidden]), "mdl", axis=1, tiled=True)
+    both_in = jnp.concatenate(
+        lax.all_to_all(
+            jnp.stack([jnp.stack([pol_hidden, ref_hidden])] * lax.axis_size("mdl")), "mdl", 0, 0
+        ),
+        axis=1,
+    )
     partials = (
         mlp_partial(both_in[0], pol_mlp_gain, pol_gate, pol_up, pol_down),
         mlp_partial(both_in[1], ref_mlp_gain, ref_gate, ref_up, ref_down),

time: 922 us -> 957 us (1.038)
  waiting for transfers between devices: 435 us -> 448 us
  starting transfers between devices: 0.3 us -> 12.6 us
    all_to_all x0 -> x1, waiting for transfers between devices: none -> 95.6 us  [per_device(): lax.all_to_all(jnp.stack([jnp.stack([pol_hidden, ref_hidden])] * lax.axis...]
    all_gather x1 -> x0, waiting for transfers between devices: 81.7 us -> none  [per_device(): lax.all_gather(jnp.stack([pol_hidden, ref_hidden]), 'mdl', axis=1, tiled=...]
    slice x1 -> x0, local copies, waits for them, and re-layouts: 13.2 us -> none  [per_device(): both_in[i].astype(jnp.float32) + mixed[i]]
    all_to_all x0 -> x1, starting transfers between devices: none -> 12.3 us  [per_device(): lax.all_to_all(jnp.stack([jnp.stack([pol_hidden, ref_hidden])] * lax.axis...]
    convert_element_type x0 -> x2, local copies, waits for them, and re-layouts: none -> 10.6 us  [per_device(): both_in[i].astype(jnp.float32) + mixed[i]]
  transfers between devices with their start and end apart: 3 -> 3, of which waited for: 3 -> 3; matrix products, arithmetic and copies ran while one was open for 1% -> 0% of each run, Pallas kernels for 0% -> 0%
where the time goes in v1:
time: 957 us; the launch traced here: 956 us
  waiting for transfers between devices  448 us (47%)
  blocking collectives  400 us (42%)
  matrix products  32.5 us (3%)
  local copies, waits for them, and re-layouts  25.3 us (3%)
  other arithmetic  23.5 us (2%)
  between operations  14.2 us (1%)
  starting transfers between devices  12.6 us (1%)
    psum x1, blocking collectives, per_device(): lax.psum((pol_terms[1] * jnp.exp(pol_terms[0] - peaks[0]), pol_terms[2],...  246 us
    psum x1, waiting for transfers between devices, per_device(): mixed = lax.psum(partials, 'mdl')  201 us
    all_gather x1, waiting for transfers between devices, per_device(): every = lax.all_gather(finals, 'grp', axis=1, tiled=True)  152 us
    pmax x2, blocking collectives, per_device(): peaks = lax.pmax(lax.pmax((pol_terms[0], ref_terms[0]), 'mdl'), 'grp')  139 us
    all_to_all x1, waiting for transfers between devices, per_device(): lax.all_to_all(jnp.stack([jnp.stack([pol_hidden, ref_hidden])] * lax.axis...  95.6 us
  transfers between devices with their start and end apart: 3, of which 3 were waited for; matrix products, arithmetic and copies ran while one was open for 0% of the time, Pallas kernels for 0%

profile of v1, /device:TPU:8, one launch (start us, length us, event | category | flops | bytes accessed | tf_op | source)
XLA Modules:
  0.0 956.4 jit_solution(10177503376572032478)
XLA Ops:
  7.2 1.0 pad_maximum_fusion.1
  8.2 4.1 stack.17
  12.2 12.3 %all-to-all-start = ((bf16[64,2,4,4096]{3,2,1,0:T(4,128)(2,1)}), bf16[64,2,4,4096]{3,2,1,0:T(4,128)(2,1)}, u32[]{:S(2)}, u32[]{:S(2)}) async-start(bf16[64,2,4,4096]{3,2,1,0:T(4,128)(2,1)} %stack.17), calls=%async_computation | async-start | bytes 8388608 | tf_op jit(solution)/shard_map/all_to_all | solution.py:61
  25.2 95.6 %all-to-all-done = bf16[64,2,4,4096]{3,2,1,0:T(4,128)(2,1)} async-done(((bf16[64,2,4,4096]{3,2,1,0:T(4,128)(2,1)}), bf16[64,2,4,4096]{3,2,1,0:T(4,128)(2,1)}, u32[]{:S(2)}, u32[]{:S(2)}) %all-to-all-start) | async-done | bytes 4194336 | tf_op jit(solution)/shard_map/all_to_all | solution.py:61
  120.8 3.9 multiply_reduce_fusion
  124.7 6.8 slice_convert_fusion
  131.5 0.6 rsqrt.41
  132.1 5.3 reshape.111
  137.4 0.7 rsqrt.39
  138.0 5.3 reshape.110
  143.3 4.4 fusion.31
  147.7 7.2 fusion.12
  154.9 4.4 fusion.30
  159.3 7.2 fusion.13
  167.2 201.0 %all-reduce.7.cloned.1.call-done = (f32[256,4096]{1,0:T(8,128)}, f32[256,4096]{1,0:T(8,128)}) async-done(((f32[256,4096]{1,0:T(8,128)}, f32[256,4096]{1,0:T(8,128)}), (f32[256,4096]{1,0:T(8,128)}, f32[256,4096]{1,0:T(8,128)})) %all-reduce.7.cloned.1.call-update) | async-done | bytes 8388624 | tf_op jit(solution)/shard_map/psum | solution.py:70
  368.3 4.3 fusion.2
  372.9 2.0 copy-done.4
  374.9 0.7 fusion.5
  375.7 0.6 fusion.9
  377.0 2.3 pad_maximum_fusion
  380.3 1.5 constant_dynamic-slice_fusion
  381.8 1.5 constant_dynamic-slice_fusion.1
  383.2 151.6 %all-gather.2.cloned.1.call-done = bf16[2,1024,4096]{2,1,0:T(8,128)(2,1)} async-done(((bf16[2,256,4096]{2,1,0:T(8,128)(2,1)}), bf16[2,1024,4096]{2,1,0:T(8,128)(2,1)}) %all-gather.2.cloned.1.call-update) | async-done | bytes 16777232 | tf_op jit(solution)/shard_map/all_gather | solution.py:74
  534.9 5.9 fusion.32
  540.8 2.2 copy-done.13
  543.6 3.4 fusion.33
  547.0 131.0 %all-reduce.2 = (f32[1024]{0:T(1024)S(1)}, f32[1024]{0:T(1024)S(1)}) all-reduce(f32[1024]{0:T(1024)S(1)} %get-tuple-element.33, f32[1024]{0:T(1024)S(1)} %get-tuple-element.31), channel_id=1, replica_groups=mesh['grp'=4,'mdl'=64] {'mdl'}, use_global_device_ids=true, to_apply=%region_21.22 | all-reduce | flops 2048 | bytes 16384 | tf_op jit(solution)/shard_map/pmax | solution.py:80
  678.0 8.4 all-reduce.4
  686.4 1.7 fusion.14
  688.2 246.2 %all-reduce = (f32[1024]{0:T(1024)S(1)}, f32[1024]{0:T(1024)S(1)}, f32[1024]{0:T(1024)S(1)}, f32[1024]{0:T(1024)S(1)}) all-reduce(f32[1024]{0:T(1024)S(1)} %exponential_multiply_fusion, f32[1024]{0:T(1024)S(1)} %get-tuple-element.10, f32[1024]{0:T(1024)S(1)} %exponential_multiply_fusion.1, ...), channel_id=1, replica_groups=mesh['grp'=4,'mdl'=64] {'mdl'}, use_global_device_ids=true, to_apply=%region_24.25 | all-reduce | flops 4096 | bytes 32768 | tf_op jit(solution)/shard_map/psum | solution.py:82
  934.3 14.6 %all-reduce.3 = (f32[1024]{0:T(1024)S(1)}, f32[1024]{0:T(1024)S(1)}, f32[1024]{0:T(1024)S(1)}, f32[1024]{0:T(1024)S(1)}) all-reduce(f32[1024]{0:T(1024)S(1)} %get-tuple-element.11, f32[1024]{0:T(1024)S(1)} %get-tuple-element.12, f32[1024]{0:T(1024)S(1)} %get-tuple-element.13, ...), channel_id=1, replica_groups=mesh['grp'=4,'mdl'=64] {'grp'}, use_global_device_ids=true, to_apply=%region_25.26 | all-reduce | flops 4096 | bytes 32768 | tf_op jit(solution)/shard_map/psum | solution.py:81
  948.9 0.6 select_reduce_fusion
  (48 shorter events, 4.0 us)
Async XLA Ops:
  7.2 527.7 %copy-start = (bf16[250,4096]{1,0:T(8,128)(2,1)S(1)}, bf16[250,4096]{1,0:T(8,128)(2,1)}, u32[]{:S(2)}) copy-start(bf16[250,4096]{1,0:T(8,128)(2,1)} %param.28) | copy-start | bytes 6144004
  12.2 12.4 %copy-start.7 = (bf16[4096]{0:T(1024)(128)(2,1)S(1)}, bf16[4096]{0:T(1024)(128)(2,1)}, u32[]{:S(2)}) copy-start(bf16[4096]{0:T(1024)(128)(2,1)} %param.19) | copy-start | bytes 24580
  12.2 13.0 %copy-start.8 = (bf16[4096]{0:T(1024)(128)(2,1)S(1)}, bf16[4096]{0:T(1024)(128)(2,1)}, u32[]{:S(2)}) copy-start(bf16[4096]{0:T(1024)(128)(2,1)} %param.18) | copy-start | bytes 24580
  12.2 108.6 %all-to-all-start = ((bf16[64,2,4,4096]{3,2,1,0:T(4,128)(2,1)}), bf16[64,2,4,4096]{3,2,1,0:T(4,128)(2,1)}, u32[]{:S(2)}, u32[]{:S(2)}) async-start(bf16[64,2,4,4096]{3,2,1,0:T(4,128)(2,1)} %stack.17), calls=%async_computation | async-start | bytes 8388608 | tf_op jit(solution)/shard_map/all_to_all | solution.py:61
  24.6 343.7 %all-reduce.7.cloned.1.call-start = ((), (), s32[]{:S(2)}) async-start(), calls=%async_computation.2 | async-start | bytes 16777216 | tf_op jit(solution)/shard_map/psum | solution.py:70
  143.3 4.4 copy-start.5
  154.9 4.4 copy-start.6
  166.5 0.7 copy-start.9
  166.5 0.7 copy-start.10
  166.6 368.3 %all-gather.2.cloned.1.call-start = ((), (), s32[]{:S(2)}) async-start(), calls=%async_computation.1 | async-start | bytes 20971520 | tf_op jit(solution)/shard_map/all_gather | solution.py:74
  368.3 4.6 copy-start.1
  368.3 6.7 copy-start.4
  372.6 3.1 copy-start.2
  375.7 1.4 copy-start.3
  379.3 0.7 copy-start.12
  534.9 8.2 copy-start.13
  534.9 8.7 copy-start.14
  543.6 142.8 %copy-start.11 = (s32[1024]{0:T(1024)S(1)}, s32[1024]{0:T(1024)}, u32[]{:S(2)}) copy-start(s32[1024]{0:T(1024)} %param.30) | copy-start | bytes 12292
Sparse Core Ops, SparseCore 0:
  166.7 201.5 all-reduce.6
  379.4 155.3 all-gather.1
